TPU v7x, 32 devices: a whole 2x2x4 slice. The times are simulated.
32 devices in a mesh: lat: 8 (over z, y), lon: 4 (over x, core).
Axes of the slice: x: 2, y: 2, z: 4, core: 2. Of those that a mesh axis runs over, the one named last changes fastest.
Arguments:
- fields: float32 [6, 32, 32, 4096], P(None, None, 'lat', 'lon'), may hold values from -6 to 6
- weights: float32 [16, 32, 4096], P(None, 'lat', 'lon'), may hold values from -2 to 2
- stencil: int32 [2, 32, 4096], P(None, 'lat', 'lon'), may hold values from -3 to 4095, as said below
- bands: float32 [6, 5, 32], replicated, may hold values from -3 to 3
Outputs:
- spectral_real: float32 [192, 32, 1280], P('lon', 'lat')
- spectral_imag: float32 [192, 32, 1280], P('lon', 'lat')
Inputs may be any that keep to these rules, and one draw needn't show every extreme that they name: stencil[0, i, j] lies in i - 3 to i; stencil[1, i, j] is (j - 16 + d) mod 4096 for some d of 0 to 29.
All inputs are finite; a program needn't handle non-finite values.
Results may differ from a plain program's by a relative error of at most 0.00007.
Values sent between devices are 32-bit elements; how exact they have to be, the bound alone decides.
No kernel may reach another device: no remote copies, remote signals or barrier semaphores. Data moves between devices by JAX's collectives and lax.ppermute only.
A program may use at most 128 MiB of HBM per device.

v0:
```python
import functools
import math

import jax
import jax.numpy as jnp
from jax import lax
from jax.experimental import pallas as pl
from jax.experimental.pallas import tpu as pltpu
from jax.sharding import PartitionSpec as P

RADIX = 64
NK = 1280
HALO = 16
ROWS_OUT = 3
TAPS = 4
LANES = 128
WINDOW = 256


def shifted(block, axis, width, dim, periodic):
    count = lax.axis_size(axis)
    forward = [(i, i + 1) for i in range(count - 1)]
    if periodic:
        forward.append((count - 1, 0))
    backward = [(target, source) for source, target in forward]
    low = lax.ppermute(
        lax.slice_in_dim(block, block.shape[dim] - width, None, axis=dim), axis, forward
    )
    high = lax.ppermute(lax.slice_in_dim(block, 0, width, axis=dim), axis, backward)
    return low, high


def spectrum(block):
    n_items, n_lines, line_len = block.shape
    highest = lax.Precision.HIGH
    folded = block.reshape(n_items * n_lines, RADIX, RADIX)
    digits = jnp.arange(RADIX, dtype=jnp.int32)
    angle_one = (
        2.0 * math.pi / RADIX * (digits[:, None] * digits[None, :] % RADIX).astype(jnp.float32)
    )
    first_table = jnp.concatenate([jnp.cos(angle_one), -jnp.sin(angle_one)], axis=1)
    partial_value = jnp.einsum("rab,ac->rbc", folded, first_table, precision=highest)
    angle_two = (
        2.0
        * math.pi
        / line_len
        * (digits[:, None] * digits[None, :] % line_len).astype(jnp.float32)
    )
    cos_two = jnp.cos(angle_two)
    sin_two = jnp.sin(angle_two)
    part_re = partial_value[..., :RADIX]
    part_im = partial_value[..., RADIX:]
    twisted = jnp.concatenate(
        [part_re * cos_two + part_im * sin_two, part_im * cos_two - part_re * sin_two], axis=-1
    )
    quotients = jnp.arange(NK // RADIX, dtype=jnp.int32)
    angle_three = (
        2.0 * math.pi / RADIX * (digits[:, None] * quotients[None, :] % RADIX).astype(jnp.float32)
    )
    with_cos = jnp.einsum("rbc,bq->rqc", twisted, jnp.cos(angle_three), precision=highest)
    with_sin = jnp.einsum("rbc,bq->rqc", twisted, jnp.sin(angle_three), precision=highest)
    scale = 1.0 / math.sqrt(line_len)
    real_part = (with_cos[..., :RADIX] + with_sin[..., RADIX:]) * scale
    imag_part = (with_cos[..., RADIX:] - with_sin[..., :RADIX]) * scale
    return (real_part.reshape(n_items, n_lines, NK), imag_part.reshape(n_items, n_lines, NK))


def interp_kernel(local, lat_rows, *refs):
    if local:
        hi_ref, lo_ref, info_ref, out_ref = refs
    else:
        hi_ref, lo_ref, info_ref, base_ref, out_ref = refs
    block = pl.program_id(0)
    start = pl.multiple_of(block * LANES, LANES)
    c_index = lax.broadcasted_iota(jnp.int32, (WINDOW, LANES), 0).astype(jnp.float32)
    j_index = lax.broadcasted_iota(jnp.int32, (WINDOW, LANES), 1).astype(jnp.float32)
    for row in range(lat_rows):
        info = info_ref[row]
        offset_r = info[16:17, :]
        offset_d = info[17:18, :]
        tap = c_index - j_index - offset_d
        masks = [tap == float(b) for b in range(TAPS)]
        if local:
            acc = jnp.zeros(out_ref.shape[1:], jnp.float32)
        else:
            acc = base_ref[row]
        for p in range(2 * ROWS_OUT + 1):
            h = row + p
            inside = ROWS_OUT <= h < ROWS_OUT + lat_rows
            if inside != local:
                continue
            if local:
                index = h - ROWS_OUT
            else:
                index = h if h < ROWS_OUT else h - lat_rows
            picked = []
            for b in range(TAPS):
                value = jnp.zeros_like(offset_r)
                for a in range(TAPS):
                    if 0 <= p - a <= ROWS_OUT:
                        value = jnp.where(offset_r == float(p - a), info[4 * a + b : 4 * a + b + 1, :], value)
                picked.append(value)
            matrix = jnp.where(
                masks[0],
                picked[0],
                jnp.where(masks[1], picked[1], jnp.where(masks[2], picked[2], jnp.where(masks[3], picked[3], 0.0))),
            )
            m_hi = matrix.astype(jnp.bfloat16)
            m_lo = (matrix - m_hi.astype(jnp.float32)).astype(jnp.bfloat16)
            x_hi = hi_ref[index, :, pl.ds(start, WINDOW)]
            x_lo = lo_ref[index, :, pl.ds(start, WINDOW)]
            acc = acc + jnp.dot(x_hi, m_hi, preferred_element_type=jnp.float32)
            acc = acc + jnp.dot(x_hi, m_lo, preferred_element_type=jnp.float32)
            acc = acc + jnp.dot(x_lo, m_hi, preferred_element_type=jnp.float32)
        out_ref[row] = acc


def interpolate(x_hi, x_lo, info, lat_rows, lon_cols, base=None):
    n_rows, n_items, width = x_hi.shape
    blocks = lon_cols // LANES
    whole = pl.BlockSpec((n_rows, n_items, width), lambda jb: (0, 0, 0))
    tile = pl.BlockSpec((lat_rows, n_items, LANES), lambda jb: (0, 0, jb))
    specs = [whole, whole, pl.BlockSpec((lat_rows, info.shape[1], LANES), lambda jb: (0, 0, jb))]
    operands = [x_hi, x_lo, info]
    if base is not None:
        specs.append(tile)
        operands.append(base)
    return pl.pallas_call(
        functools.partial(interp_kernel, base is None, lat_rows),
        out_shape=jax.ShapeDtypeStruct((lat_rows, n_items, lon_cols), jnp.float32),
        grid=(blocks,),
        in_specs=specs,
        out_specs=tile,
        compiler_params=pltpu.CompilerParams(vmem_limit_bytes=48 * 1024 * 1024),
    )(*operands)


def vertical_mix(raw, bands):
    n_levels = raw.shape[-2]
    pad = [(0, 0)] * raw.ndim
    pad[-2] = (2, 2)
    stacked = jnp.pad(raw, pad)
    lead = (None,) * (raw.ndim - 3)
    mixed = bands[lead + (slice(None), 0, slice(None), None)] * stacked[..., 0:n_levels, :]
    for shift_k in range(1, 5):
        mixed = mixed + bands[lead + (slice(None), shift_k, slice(None), None)] * stacked[
            ..., shift_k : shift_k + n_levels, :
        ]
    return mixed


def widen(block):
    left, right = shifted(block, "lon", HALO, block.ndim - 1, True)
    return jnp.concatenate([left, block, right], axis=block.ndim - 1)


def split_rows(rows, width):
    pad = [(0, 0)] * (rows.ndim - 1) + [(0, width - rows.shape[-1])]
    padded = jnp.pad(rows, pad)
    rounded = lax.reduce_precision(padded, exponent_bits=8, mantissa_bits=7)
    return rounded.astype(jnp.bfloat16), (padded - rounded).astype(jnp.bfloat16)


def on_device(fields, weights, stencil, bands):
    n_fields, n_levels, lat_rows, lon_cols = fields.shape
    n_items = n_fields * n_levels
    below_raw, above_raw = shifted(fields, "lat", ROWS_OUT, 2, False)

    width = lon_cols + LANES
    local_rows = vertical_mix(jnp.transpose(fields, (2, 0, 1, 3)), bands)
    local_hi, local_lo = split_rows(widen(local_rows.reshape(lat_rows, n_items, lon_cols)), width)

    lat_start = lax.axis_index("lat") * lat_rows
    lon_start = lax.axis_index("lon") * lon_cols
    line_len = lon_cols * lax.axis_size("lon")
    row_g = lat_start + jnp.arange(lat_rows, dtype=jnp.int32)[:, None]
    col_g = lon_start + jnp.arange(lon_cols, dtype=jnp.int32)[None, :]
    offset_r = (stencil[0] - row_g + ROWS_OUT).astype(jnp.float32)
    offset_d = jnp.mod(stencil[1] - col_g + HALO, line_len).astype(jnp.float32)
    info = jnp.concatenate(
        [
            jnp.transpose(weights, (1, 0, 2)),
            offset_r[:, None, :],
            offset_d[:, None, :],
            jnp.zeros((lat_rows, 6, lon_cols), jnp.float32),
        ],
        axis=1,
    )
    partial = interpolate(local_hi, local_lo, info, lat_rows, lon_cols)

    below_raw, above_raw, partial = lax.optimization_barrier((below_raw, above_raw, partial))
    halo_raw = jnp.concatenate([below_raw, above_raw], axis=2)
    halo_rows = vertical_mix(jnp.transpose(halo_raw, (2, 0, 1, 3)), bands)
    halo_hi, halo_lo = split_rows(widen(halo_rows.reshape(2 * ROWS_OUT, n_items, lon_cols)), width)
    departed = interpolate(halo_hi, halo_lo, info, lat_rows, lon_cols, base=partial)

    gathered = lax.all_to_all(departed, "lon", split_axis=1, concat_axis=2, tiled=True)
    real_part, imag_part = spectrum(gathered)
    return (jnp.transpose(real_part, (1, 0, 2)), jnp.transpose(imag_part, (1, 0, 2)))


def solution(mesh):
    placed = (P(None, None, "lat", "lon"), P(None, "lat", "lon"), P(None, "lat", "lon"), P())
    return jax.shard_map(
        on_device,
        mesh=mesh,
        in_specs=placed,
        out_specs=(P("lon", "lat", None), P("lon", "lat", None)),
        check_vma=False,
    )
```

profile of v0, /device:TPU:24, one launch (start us, length us, event | category | flops | bytes accessed | tf_op | source)
XLA Modules:
  0.0 232.9 jit_solution(1285874168938352268)
XLA Ops:
  0.6 5.7 %fusion.66 = (f32[6,32,3,1024]{3,2,1,0:T(4,128)S(1)}, f32[6,32,3,1024]{3,2,1,0:T(4,128)S(1)}) fusion(f32[6,32,4,1024]{3,2,1,0:T(4,128)} %param.4), kind=kLoop, calls=%fused_computation.106 | loop fusion | bytes 9437184 | tf_op jit(solution)/shard_map/slice | solution.py:29
  6.3 2.8 %copy.39 = f32[6,32,3,1024]{3,1,2,0:T(8,128)} copy(f32[6,32,3,1024]{3,2,1,0:T(4,128)S(1)} %get-tuple-element.25) | data formatting | bytes 4718592
  9.1 3.7 %collective-permute-start = (f32[6,32,3,1024]{3,1,2,0:T(8,128)}, f32[6,32,3,1024]{3,1,2,0:T(8,128)}, u32[]{:S(2)}, u32[]{:S(2)}) collective-permute-start(f32[6,32,3,1024]{3,1,2,0:T(8,128)} %copy.39), channel_id=1, source_target_pairs={{0,4},{4,8},{8,12},{12,16},{16,20},{20,24},{24,28},{1,5},{5,9},{9,... | collective-permute-start | bytes 7077896 | tf_op jit(solution)/shard_map/ppermute | solution.py:26
  12.8 2.8 %copy.40 = f32[6,32,3,1024]{3,1,2,0:T(8,128)} copy(f32[6,32,3,1024]{3,2,1,0:T(4,128)S(1)} %get-tuple-element.24) | data formatting | bytes 4718592
  15.6 3.3 %collective-permute-start.1 = (f32[6,32,3,1024]{3,1,2,0:T(8,128)}, f32[6,32,3,1024]{3,1,2,0:T(8,128)}, u32[]{:S(2)}, u32[]{:S(2)}) collective-permute-start(f32[6,32,3,1024]{3,1,2,0:T(8,128)} %copy.40), channel_id=1, source_target_pairs={{4,0},{8,4},{12,8},{16,12},{20,16},{24,20},{28,24},{5,1},{9,5},{13... | collective-permute-start | bytes 7077896 | tf_op jit(solution)/shard_map/ppermute | solution.py:29
  19.0 2.8 %multiply_add_fusion.1 = f32[4,6,32,1024]{3,0,2,1:T(4,128)S(1)} fusion(f32[4,6,32,1024]{3,0,2,1:T(4,128)S(1)} %bitcast.54, f32[6,32]{1,0:T(8,128)S(1)} %get-tuple-element.31, f32[6,32]{1,0:T(8,128)S(1)} %get-tuple-element.32, f32[6,32]{1,0:T(8,128)S(1)} %get-tuple-element.29, f32[6,32]{1,0:T(8,128)S(1)} %get-tuple-element.30, f32[6,32]{1,0:T(8,128)S(1)} %get-tuple-element.28), kind=kLoop, calls=%fused_computation.23 | loop fusion | flops 7077888 | bytes 6295296 | tf_op jit(solution)/shard_map/add | solution.py:146
  21.8 1.8 copy.24
  23.6 1.0 fusion.65
  24.6 0.4 collective-permute-start.3
  25.1 0.9 copy.60
  26.2 1.1 maximum_maximum_fusion.refs_2_
  27.3 7.1 %collective-permute-done.3 = f32[4,192,16]{2,1,0:T(8,128)} collective-permute-done((f32[4,192,16]{2,1,0:T(8,128)}, f32[4,192,16]{2,1,0:T(8,128)}, u32[]{:S(2)}, u32[]{:S(2)}) %collective-permute-start.3) | collective-permute-done | bytes 49184 | tf_op jit(solution)/shard_map/ppermute | solution.py:29
  34.3 2.1 collective-permute-done.2
  36.4 4.4 %concatenate.18 = f32[4,192,1056]{2,1,0:T(8,128)} concatenate(f32[4,192,16]{2,1,0:T(8,128)} %collective-permute-done.2, f32[4,192,1024]{2,1,0:T(8,128)S(1)} %bitcast.58, f32[4,192,16]{2,1,0:T(8,128)} %collective-permute-done.3), dimensions={2} | concatenate | bytes 6488064 | tf_op jit(solution)/shard_map/concatenate | solution.py:154
  40.8 2.6 %fusion.9 = (bf16[4,192,1152]{2,1,0:T(8,128)(2,1)S(1)}, bf16[4,192,1152]{2,1,0:T(8,128)(2,1)S(1)}) fusion(f32[4,192,1056]{2,1,0:T(8,128)} %concatenate.18), kind=kLoop, calls=%fused_computation.21 | loop fusion | flops 3538944 | bytes 6782976 | tf_op jit(solution)/shard_map/convert_element_type | solution.py:161
  43.4 13.6 %shard_map.59.refs_3_ = f32[4,192,1024]{2,1,0:T(8,128)} custom-call(bf16[4,192,1152]{2,1,0:T(8,128)(2,1)S(1)} %get-tuple-element.21.refs_0_, bf16[4,192,1152]{2,1,0:T(8,128)(2,1)S(1)} %get-tuple-element.20.refs_1_, f32[4,24,1024]{2,1,0:T(8,128)S(1)} %maximum_maximum_fusion.refs_2_), custom_call_target="tpu_custom_call" | custom-call | tf_op jit(solution)/shard_map/pallas_call | solution.py:128
  57.0 8.5 %collective-permute-done = f32[6,32,3,1024]{3,1,2,0:T(8,128)} collective-permute-done((f32[6,32,3,1024]{3,1,2,0:T(8,128)}, f32[6,32,3,1024]{3,1,2,0:T(8,128)}, u32[]{:S(2)}, u32[]{:S(2)}) %collective-permute-start) | collective-permute-done | bytes 2359328 | tf_op jit(solution)/shard_map/ppermute | solution.py:26
  65.6 50.5 %collective-permute-done.1 = f32[6,32,3,1024]{3,1,2,0:T(8,128)} collective-permute-done((f32[6,32,3,1024]{3,1,2,0:T(8,128)}, f32[6,32,3,1024]{3,1,2,0:T(8,128)}, u32[]{:S(2)}, u32[]{:S(2)}) %collective-permute-start.1) | collective-permute-done | bytes 2359328 | tf_op jit(solution)/shard_map/ppermute | solution.py:29
  116.0 2.8 %maximum_bitcast_fusion = f32[6,6,32,1024]{3,2,0,1:T(8,128)S(1)} fusion(f32[6,32,3,1024]{3,1,2,0:T(8,128)} %collective-permute-done.1, f32[6,32,3,1024]{3,1,2,0:T(8,128)} %collective-permute-done), kind=kLoop, calls=%fused_computation.20 | loop fusion | flops 1179648 | bytes 9437184 | tf_op jit(solution)/shard_map/transpose | solution.py:193
  118.8 2.9 %fusion.5 = f32[6,6,32,1024]{3,2,0,1:T(8,128)S(1)} fusion(f32[6,6,32,1024]{3,2,0,1:T(8,128)S(1)} %maximum_bitcast_fusion, f32[6,32]{1,0:T(8,128)S(1)} %get-tuple-element.31, f32[6,32]{1,0:T(8,128)S(1)} %copy-done.4, f32[6,32]{1,0:T(8,128)S(1)} %get-tuple-element.29, f32[6,32]{1,0:T(8,128)S(1)} %get-tuple-element.30, f32[6,32]{1,0:T(8,128)S(1)} %get-tuple-element.28), kind=kLoop, calls=%fused_computation.16 | loop fusion | flops 10616832 | bytes 9441024 | tf_op jit(solution)/shard_map/add | solution.py:146
  121.7 0.4 copy.28
  122.1 2.1 copy-done.1
  124.2 0.2 fusion.64
  124.4 0.2 copy.30
  124.6 1.1 collective-permute-start.5
  125.8 0.2 copy.29
  126.0 2.7 %collective-permute-done.5 = f32[6,192,16]{1,2,0:T(8,128)S(1)} collective-permute-done((f32[6,192,16]{1,2,0:T(8,128)S(1)}, f32[6,192,16]{1,2,0:T(8,128)S(1)}, u32[]{:S(2)}, u32[]{:S(2)}) %collective-permute-start.5) | collective-permute-done | bytes 73760 | tf_op jit(solution)/shard_map/ppermute | solution.py:29
  128.7 0.2 copy.32
  128.9 1.1 collective-permute-done.4
  130.1 0.2 copy.31
  130.3 6.9 %concatenate.21 = f32[6,192,1056]{2,1,0:T(8,128)} concatenate(f32[6,192,16]{2,1,0:T(8,128)S(1)} %copy.31, f32[6,192,1024]{2,1,0:T(8,128)} %bitcast.56, f32[6,192,16]{2,1,0:T(8,128)S(1)} %copy.32), dimensions={2} | concatenate | bytes 9732096 | tf_op jit(solution)/shard_map/concatenate | solution.py:154
  137.1 3.6 %fusion = (bf16[6,192,1152]{2,1,0:T(8,128)(2,1)S(1)}, bf16[6,192,1152]{2,1,0:T(8,128)(2,1)S(1)}) fusion(f32[6,192,1056]{2,1,0:T(8,128)} %concatenate.21), kind=kLoop, calls=%fused_computation.9 | loop fusion | flops 5308416 | bytes 10174464 | tf_op jit(solution)/shard_map/convert_element_type | solution.py:161
  140.7 11.7 %shard_map.60 = f32[4,192,1024]{2,1,0:T(8,128)} custom-call(bf16[6,192,1152]{2,1,0:T(8,128)(2,1)S(1)} %get-tuple-element.15.refs_0_, bf16[6,192,1152]{2,1,0:T(8,128)(2,1)S(1)} %get-tuple-element.14.refs_1_, f32[4,24,1024]{2,1,0:T(8,128)S(1)} %maximum_maximum_fusion.refs_2_, f32[4,192,1024]{2,1,0:T(8,128)} %shard_map.59.refs_3_), custom_call_target="tpu_custom_call" | custom-call | tf_op jit(solution)/shard_map/pallas_call | solution.py:128
  152.4 5.6 %copy.33 = f32[4,192,1024]{2,0,1:T(4,128)} copy(f32[4,192,1024]{2,1,0:T(8,128)} %shard_map.60) | data formatting | bytes 6291456 | tf_op jit(solution)/shard_map/pallas_call | solution.py:128
  158.0 3.9 %all-to-all-start = ((f32[4,192,1024]{2,0,1:T(4,128)}), f32[4,192,1024]{2,0,1:T(4,128)S(1)}, u32[]{:S(2)}, u32[]{:S(2)}) async-start(f32[4,192,1024]{2,0,1:T(4,128)} %copy.33), calls=%async_computation | async-start | bytes 6291456 | tf_op jit(solution)/shard_map/all_to_all | solution.py:197
  162.1 0.1 sine_negate_fusion
  162.2 36.4 %all-to-all-done = f32[4,192,1024]{2,0,1:T(4,128)S(1)} async-done(((f32[4,192,1024]{2,0,1:T(4,128)}), f32[4,192,1024]{2,0,1:T(4,128)S(1)}, u32[]{:S(2)}, u32[]{:S(2)}) %all-to-all-start) | async-done | bytes 3145760 | tf_op jit(solution)/shard_map/all_to_all | solution.py:197
  198.6 3.8 %copy.59 = f32[4,4,48,1024]{3,1,2,0:T(4,128)} copy(f32[4,4,48,1024]{3,0,2,1:T(4,128)S(1)} %bitcast.59) | data formatting | bytes 6291456 | tf_op jit(solution)/shard_map/all_to_all | solution.py:197
  202.3 6.2 %reshape.174 = f32[192,64,64]{2,1,0:T(8,128)} reshape(f32[4,48,4,1024]{3,2,1,0:T(4,128)} %bitcast.60) | data formatting | bytes 6291456 | tf_op jit(solution)/shard_map/reshape | solution.py:36
  208.5 7.3 %fusion.21 = f32[192,64,128]{2,1,0:T(8,128)S(1)} fusion(f32[192,64,64]{2,1,0:T(8,128)} %reshape.174, f32[64,64]{1,0:T(8,128)S(1)} %get-tuple-element.35, f32[64,64]{1,0:T(8,128)S(1)} %get-tuple-element.36), kind=kOutput, calls=%fused_computation.49 | convolution fusion | flops 603987968 | bytes 9469952 | tf_op jit(solution)/shard_map/rab,ac->rbc/dot_general | solution.py:42
  215.8 3.3 %multiply_add_fusion = (f32[192,64,64]{2,1,0:T(8,128)S(1)}, f32[192,64,64]{2,1,0:T(8,128)S(1)}) fusion(f32[192,64,128]{2,1,0:T(8,128)S(1)} %fusion.21, f32[64,64]{1,0:T(8,128)S(1)} %get-tuple-element.37, f32[64,64]{1,0:T(8,128)S(1)} %get-tuple-element.38), kind=kLoop, calls=%fused_computation.8 | loop fusion | flops 4718592 | bytes 12615680 | tf_op jit(solution)/shard_map/add | solution.py:54
  219.1 2.7 %fusion.16 = f32[192,20,128]{2,1,0:T(8,128)S(1)} fusion(f32[192,64,64]{2,1,0:T(8,128)S(1)} %get-tuple-element.13, f32[192,64,64]{2,1,0:T(8,128)S(1)} %get-tuple-element.12), kind=kOutput, calls=%fused_computation.33 | convolution fusion | flops 190334464 | bytes 8257536 | tf_op jit(solution)/shard_map/rbc,bq->rqc/dot_general | solution.py:61
  221.9 2.7 %fusion.15 = f32[192,20,128]{2,1,0:T(8,128)S(1)} fusion(f32[192,64,64]{2,1,0:T(8,128)S(1)} %get-tuple-element.13, f32[192,64,64]{2,1,0:T(8,128)S(1)} %get-tuple-element.12), kind=kOutput, calls=%fused_computation.32 | convolution fusion | flops 190334464 | bytes 8257536 | tf_op jit(solution)/shard_map/rbc,bq->rqc/dot_general | solution.py:60
  224.6 2.7 %fusion.11 = (f32[192,20,64]{2,1,0:T(8,128)}, f32[192,20,64]{2,1,0:T(8,128)S(1)}) fusion(f32[192,20,128]{2,1,0:T(8,128)S(1)} %fusion.16, f32[192,20,128]{2,1,0:T(8,128)S(1)} %fusion.15), kind=kLoop, calls=%fused_computation.27 | loop fusion | flops 983040 | bytes 5898240 | tf_op jit(solution)/shard_map/mul | solution.py:64
  227.3 2.0 reshape.176
  229.3 1.6 copy.37
  230.8 0.5 reshape.175
  231.3 1.6 copy.36
  (23 shorter events, 0.5 us)
Async XLA Ops:
  9.1 9.8 %copy-start.6 = (f32[6,5,32]{2,0,1:T(8,128)S(1)}, f32[6,5,32]{2,0,1:T(8,128)}, u32[]{:S(2)}) copy-start(f32[6,5,32]{2,0,1:T(8,128)} %param.7) | copy-start | bytes 11524
  9.1 9.9 %copy-start = (f32[6,32,4,1024]{3,2,1,0:T(4,128)S(1)}, f32[6,32,4,1024]{3,2,1,0:T(4,128)}, u32[]{:S(2)}) copy-start(f32[6,32,4,1024]{3,2,1,0:T(4,128)} %param.4) | copy-start | bytes 9437188
  9.1 56.5 %collective-permute-start = (f32[6,32,3,1024]{3,1,2,0:T(8,128)}, f32[6,32,3,1024]{3,1,2,0:T(8,128)}, u32[]{:S(2)}, u32[]{:S(2)}) collective-permute-start(f32[6,32,3,1024]{3,1,2,0:T(8,128)} %copy.39), channel_id=1, source_target_pairs={{0,4},{4,8},{8,12},{12,16},{16,20},{20,24},{24,28},{1,5},{5,9},{9,... | collective-permute-start | bytes 7077896 | tf_op jit(solution)/shard_map/ppermute | solution.py:26
  15.6 100.4 %collective-permute-start.1 = (f32[6,32,3,1024]{3,1,2,0:T(8,128)}, f32[6,32,3,1024]{3,1,2,0:T(8,128)}, u32[]{:S(2)}, u32[]{:S(2)}) collective-permute-start(f32[6,32,3,1024]{3,1,2,0:T(8,128)} %copy.40), channel_id=1, source_target_pairs={{4,0},{8,4},{12,8},{16,12},{20,16},{24,20},{28,24},{5,1},{9,5},{13... | collective-permute-start | bytes 7077896 | tf_op jit(solution)/shard_map/ppermute | solution.py:29
  19.0 4.7 %copy-start.3 = (f32[6,32]{1,0:T(8,128)}, f32[6,32]{1,0:T(8,128)S(1)}, u32[]{:S(2)}) copy-start(f32[6,32]{1,0:T(8,128)S(1)} %get-tuple-element.32) | copy-start | bytes 2308
  21.8 3.4 %copy-start.2 = (f32[16,4,1024]{2,1,0:T(4,128)S(1)}, f32[16,4,1024]{2,1,0:T(4,128)}, u32[]{:S(2)}) copy-start(f32[16,4,1024]{2,1,0:T(4,128)} %param.5) | copy-start | bytes 786436
  21.8 4.3 %copy-start.5 = (s32[2,4,1024]{2,1,0:T(4,128)S(1)}, s32[2,4,1024]{2,1,0:T(4,128)}, u32[]{:S(2)}) copy-start(s32[2,4,1024]{2,1,0:T(4,128)} %param.6) | copy-start | bytes 98308
  24.6 9.7 %collective-permute-start.3 = (f32[4,192,16]{2,1,0:T(8,128)}, f32[4,192,16]{2,1,0:T(8,128)}, u32[]{:S(2)}, u32[]{:S(2)}) collective-permute-start(f32[4,192,16]{2,1,0:T(8,128)} %get-tuple-element.22), channel_id=1, source_target_pairs={{1,0},{2,1},{3,2},{0,3},{5,4},{6,5},{7,6},{4,7},{9,8},{10,9},{11,1... | collective-permute-start | bytes 147464 | tf_op jit(solution)/shard_map/ppermute | solution.py:29
  25.0 11.4 %collective-permute-start.2 = (f32[4,192,16]{2,1,0:T(8,128)}, f32[4,192,16]{2,1,0:T(8,128)}, u32[]{:S(2)}, u32[]{:S(2)}) collective-permute-start(f32[4,192,16]{2,1,0:T(8,128)} %get-tuple-element.23), channel_id=1, source_target_pairs={{0,1},{1,2},{2,3},{3,0},{4,5},{5,6},{6,7},{7,4},{8,9},{9,10},{10,1... | collective-permute-start | bytes 147464 | tf_op jit(solution)/shard_map/ppermute | solution.py:26
  57.0 61.8 %copy-start.4 = (f32[6,32]{1,0:T(8,128)S(1)}, f32[6,32]{1,0:T(8,128)}, u32[]{:S(2)}) copy-start(f32[6,32]{1,0:T(8,128)} %copy-done.3) | copy-start | bytes 2308
  122.1 2.1 copy-start.1
  124.6 4.1 %collective-permute-start.5 = (f32[6,192,16]{1,2,0:T(8,128)S(1)}, f32[6,192,16]{1,2,0:T(8,128)S(1)}, u32[]{:S(2)}, u32[]{:S(2)}) collective-permute-start(f32[6,192,16]{1,2,0:T(8,128)S(1)} %copy.30), channel_id=1, source_target_pairs={{1,0},{2,1},{3,2},{0,3},{5,4},{6,5},{7,6},{4,7},{9,8},{10,9},{11,1... | collective-permute-start | bytes 221192 | tf_op jit(solution)/shard_map/ppermute | solution.py:29
  126.0 4.1 %collective-permute-start.4 = (f32[6,192,16]{1,2,0:T(8,128)S(1)}, f32[6,192,16]{1,2,0:T(8,128)S(1)}, u32[]{:S(2)}, u32[]{:S(2)}) collective-permute-start(f32[6,192,16]{1,2,0:T(8,128)S(1)} %copy.29), channel_id=1, source_target_pairs={{0,1},{1,2},{2,3},{3,0},{4,5},{5,6},{6,7},{7,4},{8,9},{9,10},{10,1... | collective-permute-start | bytes 221192 | tf_op jit(solution)/shard_map/ppermute | solution.py:26
  158.0 40.6 %all-to-all-start = ((f32[4,192,1024]{2,0,1:T(4,128)}), f32[4,192,1024]{2,0,1:T(4,128)S(1)}, u32[]{:S(2)}, u32[]{:S(2)}) async-start(f32[4,192,1024]{2,0,1:T(4,128)} %copy.33), calls=%async_computation | async-start | bytes 6291456 | tf_op jit(solution)/shard_map/all_to_all | solution.py:197
where the time goes:
time: 234 us; the launch traced here: 233 us
  waiting for transfers between devices  108 us (46%)
  local copies, waits for them, and re-layouts  51 us (22%)
  Pallas kernels  25.3 us (11%)
  other arithmetic  22.1 us (9%)
  matrix products  12.7 us (5%)
  starting transfers between devices  12.6 us (5%)
    ppermute x3, waiting for transfers between devices, shifted(): lax.ppermute(lax.slice_in_dim(block, 0, width, axis=dim), axis, backward)  60.2 us
    all_to_all x1, waiting for transfers between devices, on_device(): lax.all_to_all(departed, 'lon', split_axis=1, concat_axis=2, tiled=True)  36.4 us
    pallas_call x2, Pallas kernels, interpolate(): pl.pallas_call(functools.partial(interp_kernel, base is None, lat_rows),...  25.3 us
    unnamed x19, local copies, waits for them, and re-layouts  11.7 us
    ppermute x3, waiting for transfers between devices, shifted(): lax.ppermute(lax.slice_in_dim(block, block.shape[dim] - width, None, axis...  11.7 us
    concatenate x2, local copies, waits for them, and re-layouts, widen(): return jnp.concatenate([left, block, right], axis=block.ndim - 1)  11.2 us
    dot_general x1, matrix products, spectrum(): jnp.einsum('rab,ac->rbc', folded, first_table, precision=highest)  7.28 us
    slice x4, local copies, waits for them, and re-layouts, shifted(): lax.slice_in_dim(block, 0, width, axis=dim)  7.14 us
  transfers between devices with their start and end apart: 7, of which 7 were waited for; matrix products, arithmetic and copies ran while one was open for 8% of the time, Pallas kernels for 6%

commit v1 on v0

--- a/solution.py
+++ b/solution.py
@@ -164,11 +164,11 @@
 def on_device(fields, weights, stencil, bands):
     n_fields, n_levels, lat_rows, lon_cols = fields.shape
     n_items = n_fields * n_levels
-    below_raw, above_raw = shifted(fields, "lat", ROWS_OUT, 2, False)
-
     width = lon_cols + LANES
     local_rows = vertical_mix(jnp.transpose(fields, (2, 0, 1, 3)), bands)
-    local_hi, local_lo = split_rows(widen(local_rows.reshape(lat_rows, n_items, lon_cols)), width)
+    wide = widen(local_rows.reshape(lat_rows, n_items, lon_cols))
+    below_wide, above_wide = shifted(wide, "lat", ROWS_OUT, 0, False)
+    local_hi, local_lo = split_rows(wide, width)
 
     lat_start = lax.axis_index("lat") * lat_rows
     lon_start = lax.axis_index("lon") * lon_cols
@@ -188,10 +188,8 @@
     )
     partial = interpolate(local_hi, local_lo, info, lat_rows, lon_cols)
 
-    below_raw, above_raw, partial = lax.optimization_barrier((below_raw, above_raw, partial))
-    halo_raw = jnp.concatenate([below_raw, above_raw], axis=2)
-    halo_rows = vertical_mix(jnp.transpose(halo_raw, (2, 0, 1, 3)), bands)
-    halo_hi, halo_lo = split_rows(widen(halo_rows.reshape(2 * ROWS_OUT, n_items, lon_cols)), width)
+    below_wide, above_wide, partial = lax.optimization_barrier((below_wide, above_wide, partial))
+    halo_hi, halo_lo = split_rows(jnp.concatenate([below_wide, above_wide], axis=0), width)
     departed = interpolate(halo_hi, halo_lo, info, lat_rows, lon_cols, base=partial)
 
     gathered = lax.all_to_all(departed, "lon", split_axis=1, concat_axis=2, tiled=True)

time: 234 us -> 245 us (1.047)
  waiting for transfers between devices: 108 us -> 140 us
  local copies, waits for them, and re-layouts: 51 us -> 33.8 us
  other arithmetic: 22.1 us -> 18.9 us
    ppermute x3 -> x2, waiting for transfers between devices: 60.2 us -> 103 us  [shifted(): lax.ppermute(lax.slice_in_dim(block, 0, width, axis=dim), axis, backward)]
    ppermute x3 -> x2, waiting for transfers between devices: 11.7 us -> 0.43 us  [shifted(): lax.ppermute(lax.slice_in_dim(block, block.shape[dim] - width, None, axis...]
    concatenate x2 -> x1, local copies, waits for them, and re-layouts: 11.2 us -> 3.84 us  [widen(): return jnp.concatenate([left, block, right], axis=block.ndim - 1)]
    unnamed x19 -> x7, local copies, waits for them, and re-layouts: 11.7 us -> 5.72 us
    slice x4 -> x2, local copies, waits for them, and re-layouts: 7.14 us -> 2.88 us  [shifted(): lax.slice_in_dim(block, 0, width, axis=dim)]
    transpose x1 -> x0, other arithmetic: 2.75 us -> none  [on_device(): halo_rows = vertical_mix(jnp.transpose(halo_raw, (2, 0, 1, 3)), bands)]
    convert_element_type x2, other arithmetic: 6.2 us -> 3.7 us  [split_rows(): (padded - rounded).astype(jnp.bfloat16)]
    add x2 -> x1, other arithmetic: 5.68 us -> 7.79 us  [vertical_mix(): mixed + bands[lead + (slice(None), shift_k, slice(None), None)] * stacked...]
  transfers between devices with their start and end apart: 7 -> 5, of which waited for: 7 -> 4; matrix products, arithmetic and copies ran while one was open for 8% -> 2% of each run, Pallas kernels for 6% -> 6%
where the time goes in v1:
time: 245 us; the launch traced here: 243 us
  waiting for transfers between devices  140 us (57%)
  local copies, waits for them, and re-layouts  33.8 us (14%)
  Pallas kernels  25.3 us (10%)
  other arithmetic  18.9 us (8%)
  matrix products  12.7 us (5%)
  starting transfers between devices  12.3 us (5%)
    ppermute x2, waiting for transfers between devices, shifted(): lax.ppermute(lax.slice_in_dim(block, 0, width, axis=dim), axis, backward)  103 us
    all_to_all x1, waiting for transfers between devices, on_device(): lax.all_to_all(departed, 'lon', split_axis=1, concat_axis=2, tiled=True)  36.7 us
    pallas_call x2, Pallas kernels, interpolate(): pl.pallas_call(functools.partial(interp_kernel, base is None, lat_rows),...  25.3 us
    add x1, other arithmetic, vertical_mix(): mixed + bands[lead + (slice(None), shift_k, slice(None), None)] * stacked...  7.79 us
    dot_general x1, matrix products, spectrum(): jnp.einsum('rab,ac->rbc', folded, first_table, precision=highest)  7.28 us
    reshape x1, local copies, waits for them, and re-layouts, spectrum(): folded = block.reshape(n_items * n_lines, RADIX, RADIX)  6.22 us
    unnamed x7, local copies, waits for them, and re-layouts  5.72 us
    pallas_call x1, local copies, waits for them, and re-layouts, interpolate(): pl.pallas_call(functools.partial(interp_kernel, base is None, lat_rows),...  5.56 us
  transfers between devices with their start and end apart: 5, of which 4 were waited for; matrix products, arithmetic and copies ran while one was open for 2% of the time, Pallas kernels for 6%

profile of v1, /device:TPU:24, one launch (start us, length us, event | category | flops | bytes accessed | tf_op | source)
XLA Modules:
  0.0 243.3 jit_solution(17074975760570200013)
XLA Ops:
  0.6 0.8 slice_bitcast_fusion.4
  1.4 7.8 %multiply_add_fusion.1 = f32[4,6,32,1024]{3,0,2,1:T(4,128)S(1)} fusion(f32[4,6,32,1024]{3,0,2,1:T(4,128)} %bitcast.57, f32[6,32]{1,0:T(8,128)S(1)} %get-tuple-element.29, f32[6,32]{1,0:T(8,128)S(1)} %get-tuple-element.30, f32[6,32]{1,0:T(8,128)S(1)} %get-tuple-element.27, f32[6,32]{1,0:T(8,128)S(1)} %get-tuple-element.28, f32[6,32]{1,0:T(8,128)S(1)} %get-tuple-element.26), kind=kLoop, calls=%fused_computation.12 | loop fusion | flops 7077888 | bytes 6295296 | tf_op jit(solution)/shard_map/add | solution.py:146
  9.2 1.8 copy.20
  11.0 0.0 copy-start
  11.0 0.2 fusion.57
  11.2 1.0 collective-permute-start.1
  12.2 0.0 collective-permute-start
  12.2 9.5 %collective-permute-done.1 = f32[4,192,16]{2,1,0:T(8,128)S(1)} collective-permute-done((f32[4,192,16]{2,1,0:T(8,128)S(1)}, f32[4,192,16]{2,1,0:T(8,128)S(1)}, u32[]{:S(2)}, u32[]{:S(2)}) %collective-permute-start.1) | collective-permute-done | bytes 49184 | tf_op jit(solution)/shard_map/ppermute | solution.py:29
  21.7 0.0 copy-done
  21.7 0.0 copy-start.1
  21.7 0.7 copy-done.1
  22.4 0.4 collective-permute-done
  22.8 3.8 %concatenate.15 = f32[4,192,1056]{2,1,0:T(8,128)S(1)} concatenate(f32[4,192,16]{2,1,0:T(8,128)} %collective-permute-done, f32[4,192,1024]{2,1,0:T(8,128)} %bitcast.52, f32[4,192,16]{2,1,0:T(8,128)} %copy-done.1), dimensions={2} | concatenate | bytes 6488064 | tf_op jit(solution)/shard_map/concatenate | solution.py:154
  26.7 2.7 %fusion.56 = (f32[3,192,1056]{2,1,0:T(8,128)}, f32[3,192,1056]{2,1,0:T(8,128)}) fusion(f32[4,192,1056]{2,1,0:T(8,128)S(1)} %concatenate.15), kind=kLoop, calls=%fused_computation.93 | loop fusion | bytes 9732096 | tf_op jit(solution)/shard_map/slice | solution.py:29
  29.4 3.3 %collective-permute-start.3 = (f32[3,192,1056]{2,1,0:T(8,128)}, f32[3,192,1056]{2,1,0:T(8,128)}, u32[]{:S(2)}, u32[]{:S(2)}) collective-permute-start(f32[3,192,1056]{2,1,0:T(8,128)} %get-tuple-element.20), channel_id=1, source_target_pairs={{4,0},{8,4},{12,8},{16,12},{20,16},{24,20},{28,24},{5,1},{9,5},{13... | collective-permute-start | bytes 7299080 | tf_op jit(solution)/shard_map/ppermute | solution.py:29
  32.7 4.1 %collective-permute-start.2 = (f32[3,192,1056]{2,1,0:T(8,128)}, f32[3,192,1056]{2,1,0:T(8,128)}, u32[]{:S(2)}, u32[]{:S(2)}) collective-permute-start(f32[3,192,1056]{2,1,0:T(8,128)} %get-tuple-element.21), channel_id=1, source_target_pairs={{0,4},{4,8},{8,12},{12,16},{16,20},{20,24},{24,28},{1,5},{5,9},{9,... | collective-permute-start | bytes 7299080 | tf_op jit(solution)/shard_map/ppermute | solution.py:26
  36.8 1.8 copy.49
  38.6 0.1 pad.24.clone
  38.7 0.7 fusion.58
  39.5 0.1 fusion.23
  39.5 1.1 maximum_maximum_fusion.refs_2_
  40.6 0.6 fusion.1
  41.2 13.6 %shard_map.59.refs_3_ = f32[4,192,1024]{2,1,0:T(8,128)} custom-call(bf16[4,192,1152]{2,1,0:T(8,128)(2,1)S(1)} %get-tuple-element.19.refs_0_, bf16[4,192,1152]{2,1,0:T(8,128)(2,1)S(1)} %get-tuple-element.18.refs_1_, f32[4,24,1024]{2,1,0:T(8,128)S(1)} %maximum_maximum_fusion.refs_2_), custom_call_target="tpu_custom_call" | custom-call | tf_op jit(solution)/shard_map/pallas_call | solution.py:128
  54.9 93.1 %collective-permute-done.3 = f32[3,192,1056]{2,1,0:T(8,128)} collective-permute-done((f32[3,192,1056]{2,1,0:T(8,128)}, f32[3,192,1056]{2,1,0:T(8,128)}, u32[]{:S(2)}, u32[]{:S(2)}) %collective-permute-start.3) | collective-permute-done | bytes 2433056 | tf_op jit(solution)/shard_map/ppermute | solution.py:29
  147.9 0.0 collective-permute-done.2
  147.9 3.1 %fusion = (bf16[6,192,1152]{2,1,0:T(8,128)(2,1)S(1)}, bf16[6,192,1152]{2,1,0:T(8,128)(2,1)S(1)}) fusion(f32[3,192,1056]{2,1,0:T(8,128)} %collective-permute-done.3, f32[3,192,1056]{2,1,0:T(8,128)} %collective-permute-done.2), kind=kLoop, calls=%fused_computation.5 | loop fusion | flops 10616832 | bytes 10174464 | tf_op jit(solution)/shard_map/convert_element_type | solution.py:161
  151.0 11.7 %shard_map.60 = f32[4,192,1024]{2,1,0:T(8,128)} custom-call(bf16[6,192,1152]{2,1,0:T(8,128)(2,1)S(1)} %get-tuple-element.15.refs_0_, bf16[6,192,1152]{2,1,0:T(8,128)(2,1)S(1)} %get-tuple-element.14.refs_1_, f32[4,24,1024]{2,1,0:T(8,128)S(1)} %maximum_maximum_fusion.refs_2_, f32[4,192,1024]{2,1,0:T(8,128)} %shard_map.59.refs_3_), custom_call_target="tpu_custom_call" | custom-call | tf_op jit(solution)/shard_map/pallas_call | solution.py:128
  162.7 5.6 %copy.24 = f32[4,192,1024]{2,0,1:T(4,128)} copy(f32[4,192,1024]{2,1,0:T(8,128)} %shard_map.60) | data formatting | bytes 6291456 | tf_op jit(solution)/shard_map/pallas_call | solution.py:128
  168.2 3.9 %all-to-all-start = ((f32[4,192,1024]{2,0,1:T(4,128)}), f32[4,192,1024]{2,0,1:T(4,128)S(1)}, u32[]{:S(2)}, u32[]{:S(2)}) async-start(f32[4,192,1024]{2,0,1:T(4,128)} %copy.24), calls=%async_computation | async-start | bytes 6291456 | tf_op jit(solution)/shard_map/all_to_all | solution.py:195
  172.1 0.1 fusion.30
  172.3 0.1 sine_negate_fusion
  172.4 36.7 %all-to-all-done = f32[4,192,1024]{2,0,1:T(4,128)S(1)} async-done(((f32[4,192,1024]{2,0,1:T(4,128)}), f32[4,192,1024]{2,0,1:T(4,128)S(1)}, u32[]{:S(2)}, u32[]{:S(2)}) %all-to-all-start) | async-done | bytes 3145760 | tf_op jit(solution)/shard_map/all_to_all | solution.py:195
  209.1 3.7 %copy.48 = f32[4,4,48,1024]{3,1,2,0:T(4,128)} copy(f32[4,4,48,1024]{3,0,2,1:T(4,128)S(1)} %bitcast.53) | data formatting | bytes 6291456 | tf_op jit(solution)/shard_map/all_to_all | solution.py:195
  212.8 6.2 %reshape.170 = f32[192,64,64]{2,1,0:T(8,128)} reshape(f32[4,48,4,1024]{3,2,1,0:T(4,128)} %bitcast.54) | data formatting | bytes 6291456 | tf_op jit(solution)/shard_map/reshape | solution.py:36
  219.0 7.3 %fusion.13 = f32[192,64,128]{2,1,0:T(8,128)S(1)} fusion(f32[192,64,64]{2,1,0:T(8,128)} %reshape.170, f32[64,64]{1,0:T(8,128)S(1)} %get-tuple-element.33, f32[64,64]{1,0:T(8,128)S(1)} %get-tuple-element.34), kind=kOutput, calls=%fused_computation.38 | convolution fusion | flops 603987968 | bytes 9469952 | tf_op jit(solution)/shard_map/rab,ac->rbc/dot_general | solution.py:42
  226.3 3.2 %multiply_add_fusion = (f32[192,64,64]{2,1,0:T(8,128)S(1)}, f32[192,64,64]{2,1,0:T(8,128)S(1)}) fusion(f32[192,64,128]{2,1,0:T(8,128)S(1)} %fusion.13, f32[64,64]{1,0:T(8,128)S(1)} %get-tuple-element.35, f32[64,64]{1,0:T(8,128)S(1)} %get-tuple-element.36), kind=kLoop, calls=%fused_computation.4 | loop fusion | flops 4718592 | bytes 12615680 | tf_op jit(solution)/shard_map/add | solution.py:54
  229.6 2.7 %fusion.8 = f32[192,20,128]{2,1,0:T(8,128)S(1)} fusion(f32[192,64,64]{2,1,0:T(8,128)S(1)} %get-tuple-element.13, f32[192,64,64]{2,1,0:T(8,128)S(1)} %get-tuple-element.12), kind=kOutput, calls=%fused_computation.22 | convolution fusion | flops 190334464 | bytes 8257536 | tf_op jit(solution)/shard_map/rbc,bq->rqc/dot_general | solution.py:61
  232.3 2.7 %fusion.7 = f32[192,20,128]{2,1,0:T(8,128)S(1)} fusion(f32[192,64,64]{2,1,0:T(8,128)S(1)} %get-tuple-element.13, f32[192,64,64]{2,1,0:T(8,128)S(1)} %get-tuple-element.12), kind=kOutput, calls=%fused_computation.21 | convolution fusion | flops 190334464 | bytes 8257536 | tf_op jit(solution)/shard_map/rbc,bq->rqc/dot_general | solution.py:60
  235.0 2.7 %fusion.3 = (f32[192,20,64]{2,1,0:T(8,128)}, f32[192,20,64]{2,1,0:T(8,128)S(1)}) fusion(f32[192,20,128]{2,1,0:T(8,128)S(1)} %fusion.8, f32[192,20,128]{2,1,0:T(8,128)S(1)} %fusion.7), kind=kLoop, calls=%fused_computation.16 | loop fusion | flops 983040 | bytes 5898240 | tf_op jit(solution)/shard_map/mul | solution.py:64
  237.7 2.0 reshape.172
  239.7 1.6 copy.28
  241.3 0.5 reshape.171
  241.8 1.6 copy.27
  (3 shorter events, 0.0 us)
Async XLA Ops:
  11.0 10.6 %copy-start = (f32[4,6,32,1024]{3,2,1,0:T(8,128)}, f32[4,6,32,1024]{3,2,1,0:T(8,128)S(1)}, u32[]{:S(2)}) copy-start(f32[4,6,32,1024]{3,2,1,0:T(8,128)S(1)} %copy.20) | copy-start | bytes 9437188
  11.2 10.4 %collective-permute-start.1 = (f32[4,192,16]{2,1,0:T(8,128)S(1)}, f32[4,192,16]{2,1,0:T(8,128)S(1)}, u32[]{:S(2)}, u32[]{:S(2)}) collective-permute-start(f32[4,192,16]{2,1,0:T(8,128)S(1)} %get-tuple-element.22), channel_id=1, source_target_pairs={{1,0},{2,1},{3,2},{0,3},{5,4},{6,5},{7,6},{4,7},{9,8},{10,9},{11,1... | collective-permute-start | bytes 147464 | tf_op jit(solution)/shard_map/ppermute | solution.py:29
  12.2 10.6 %collective-permute-start = (f32[4,192,16]{2,1,0:T(8,128)S(1)}, f32[4,192,16]{2,1,0:T(8,128)}, u32[]{:S(2)}, u32[]{:S(2)}) collective-permute-start(f32[4,192,16]{2,1,0:T(8,128)S(1)} %get-tuple-element.23), channel_id=1, source_target_pairs={{0,1},{1,2},{2,3},{3,0},{4,5},{5,6},{6,7},{7,4},{8,9},{9,10},{10,1... | collective-permute-start | bytes 147464 | tf_op jit(solution)/shard_map/ppermute | solution.py:26
  21.7 0.7 copy-start.1
  29.4 118.5 %collective-permute-start.3 = (f32[3,192,1056]{2,1,0:T(8,128)}, f32[3,192,1056]{2,1,0:T(8,128)}, u32[]{:S(2)}, u32[]{:S(2)}) collective-permute-start(f32[3,192,1056]{2,1,0:T(8,128)} %get-tuple-element.20), channel_id=1, source_target_pairs={{4,0},{8,4},{12,8},{16,12},{20,16},{24,20},{28,24},{5,1},{9,5},{13... | collective-permute-start | bytes 7299080 | tf_op jit(solution)/shard_map/ppermute | solution.py:29
  32.7 115.2 %collective-permute-start.2 = (f32[3,192,1056]{2,1,0:T(8,128)}, f32[3,192,1056]{2,1,0:T(8,128)}, u32[]{:S(2)}, u32[]{:S(2)}) collective-permute-start(f32[3,192,1056]{2,1,0:T(8,128)} %get-tuple-element.21), channel_id=1, source_target_pairs={{0,4},{4,8},{8,12},{12,16},{16,20},{20,24},{24,28},{1,5},{5,9},{9,... | collective-permute-start | bytes 7299080 | tf_op jit(solution)/shard_map/ppermute | solution.py:26
  168.2 40.9 %all-to-all-start = ((f32[4,192,1024]{2,0,1:T(4,128)}), f32[4,192,1024]{2,0,1:T(4,128)S(1)}, u32[]{:S(2)}, u32[]{:S(2)}) async-start(f32[4,192,1024]{2,0,1:T(4,128)} %copy.24), calls=%async_computation | async-start | bytes 6291456 | tf_op jit(solution)/shard_map/all_to_all | solution.py:195
